TPU v7x, 256 devices: a whole 4x4x8 slice. The times are simulated.
256 devices in a mesh: con: 4 (over z_hi), grid: 64 (over z_lo, y, x, core).
Axes of the slice: x: 4, y: 4, z: 8 (z_hi: 4, z_lo: 2; z = z_hi * 2 + z_lo), core: 2. Of those that a mesh axis runs over, the one named last changes fastest.
Arguments:
- velocity: bfloat16 [8, 2, 4096, 4096], P('con', None, 'grid'), may hold values from -6 to 6
- seed_adjoint: bfloat16 [8, 2, 4096, 4096], P('con', None, 'grid'), may hold values from -6 to 6
- land_mask: int32 [4096, 4096], P('grid'), may hold values from 0 to 2
- inv_x: bfloat16 [32, 128, 128], replicated, may hold values from -0.5 to 0.5
- inv_y: bfloat16 [32, 128, 128], replicated, may hold values from -0.5 to 0.5
- weights: float32 [8], P('con'), may hold values from 0.05 to 0.5
Outputs:
- velocity_adjoint: float32 [8, 2, 4096, 4096], P('con', None, 'grid')
Inputs may be any that keep to these rules, and one draw needn't show every extreme that they name: `land_mask`: 0 marks land, 1 a wet interior cell, 2 an open-boundary cell whose value is prescribed.
All inputs are finite; a program needn't handle non-finite values.
Results may differ from a plain program's by a relative error of at most 0.0039.
Values may be sent and summed in bfloat16 or wider, within the bound.
No kernel may reach another device: no remote copies, remote signals or barrier semaphores. Data moves between devices by JAX's collectives and lax.ppermute only.
A program may use at most 64 MiB of HBM per device.

v0:
```python
import jax
import jax.numpy as jnp
from jax import lax
from jax.sharding import PartitionSpec as P

BLK = 128


def local(velocity, seed_adjoint, land_mask, inv_x, inv_y, weights):
    nblocks = inv_x.shape[0]
    con_local = velocity.shape[0]
    cols_local = seed_adjoint.shape[2]
    full_side = seed_adjoint.shape[3]
    rows_local = velocity.shape[2]
    vel_float = velocity.astype(jnp.float32)
    weight_full = weights[:, None, None, None]
    local_squares = jnp.sum(weight_full * vel_float * vel_float, axis=(0, 1))
    squares = lax.psum(local_squares, "con")
    sea_bool = land_mask == 1
    sea_float = sea_bool.astype(jnp.float32)
    sea_turned = jnp.swapaxes(sea_bool, 0, 1).astype(jnp.bfloat16)
    blocks_x = seed_adjoint.reshape(con_local, 2, cols_local, nblocks, BLK)
    across = jnp.einsum("cpyki,kji->cpykj", blocks_x, inv_x, preferred_element_type=jnp.float32)
    across = across.astype(jnp.bfloat16).reshape(con_local, 2, cols_local, full_side)
    arrived = lax.all_to_all(across, "grid", split_axis=3, concat_axis=2, tiled=True)
    count = arrived.shape[0]
    masked = arrived * sea_turned[None, None]
    blocks_y = masked.reshape(count, 2, nblocks, BLK, rows_local)
    solved = jnp.einsum("cpkiu,kji->cpukj", blocks_y, inv_y, preferred_element_type=jnp.float32)
    rhs_adjoint = solved.reshape(count, 2, rows_local, nblocks * BLK)
    local_inner = jnp.sum(rhs_adjoint * vel_float, axis=(0, 1))
    inner = lax.psum(local_inner.astype(jnp.bfloat16), "con").astype(jnp.float32)
    speed = jnp.sqrt(0.25 + squares)
    first = -0.5 * sea_float * speed * rhs_adjoint
    second = -0.5 * sea_float * weight_full * vel_float * inner / speed
    return first + second


def solution(mesh):
    return jax.shard_map(
        local,
        mesh=mesh,
        in_specs=(
            P("con", None, "grid", None),
            P("con", None, "grid", None),
            P("grid", None),
            P(),
            P(),
            P("con"),
        ),
        out_specs=P("con", None, "grid", None),
        check_vma=False,
    )
```

profile of v0, /device:TPU:1, one launch (start us, length us, event | category | flops | bytes accessed | tf_op | source)
XLA Modules:
  0.0 237.2 jit_solution(3635252358337494409)
XLA Ops:
  6.5 1.6 copy-done
  8.1 3.3 %convert_bitcast_fusion = bf16[2,2,64,32,128]{4,2,1,0,3:T(8,128)(2,1)} fusion(bf16[32,128,128]{2,1,0:T(8,128)(2,1)} %param.9, bf16[2,2,64,4096]{3,2,1,0:T(8,128)(2,1)S(1)} %copy-done), kind=kOutput, calls=%fused_computation.16 | convolution fusion | flops 269484032 | bytes 5242880 | tf_op jit(solution)/shard_map/cpyki,kji->cpykj/dot_general | solution.py:23
  11.4 10.0 %copy.22 = bf16[2,2,64,32,128]{2,1,0,4,3:T(2,128)(2,1)} copy(bf16[2,2,64,32,128]{4,2,1,0,3:T(8,128)(2,1)} %convert_bitcast_fusion) | data formatting | bytes 4194304 | tf_op jit(solution)/shard_map/reshape | solution.py:24
  21.4 9.8 %reshape.31 = bf16[64,2,8192]{2,1,0:T(2,128)(2,1)} reshape(bf16[4096,2,2,64]{3,2,1,0:T(2,128)(2,1)} %bitcast.46) | data formatting | bytes 4194304
  31.3 10.5 %all-to-all-start = ((bf16[64,2,8192]{2,1,0:T(2,128)(2,1)}), bf16[64,2,8192]{2,1,0:T(2,128)(2,1)}, u32[]{:S(2)}, u32[]{:S(2)}) async-start(bf16[64,2,8192]{2,1,0:T(2,128)(2,1)} %reshape.31), calls=%async_computation | async-start | bytes 4194304 | tf_op jit(solution)/shard_map/all_to_all | solution.py:25
  41.8 0.2 all-reduce.5.cloned.1.call-start
  42.0 1.4 broadcast_select_fusion
  43.6 0.9 copy.26
  44.5 24.8 %all-to-all-done = bf16[64,2,8192]{2,1,0:T(2,128)(2,1)} async-done(((bf16[64,2,8192]{2,1,0:T(2,128)(2,1)}), bf16[64,2,8192]{2,1,0:T(2,128)(2,1)}, u32[]{:S(2)}, u32[]{:S(2)}) %all-to-all-start) | async-done | bytes 2097184 | tf_op jit(solution)/shard_map/all_to_all | solution.py:25
  69.2 9.8 %reshape.32 = bf16[4096,2,2,64]{3,2,1,0:T(2,128)(2,1)} reshape(bf16[64,2,8192]{2,1,0:T(2,128)(2,1)} %all-to-all-done) | data formatting | bytes 4194304
  79.0 6.8 %copy.38 = bf16[2,2,64,64,64]{2,3,4,1,0:T(8,128)(2,1)} copy(bf16[2,2,64,64,64]{2,1,0,4,3:T(2,128)(2,1)} %bitcast.47) | data formatting | bytes 4194304 | tf_op jit(solution)/shard_map/all_to_all | solution.py:25
  85.8 6.2 %all_to_all.16 = bf16[2,2,32,128,64]{3,2,4,1,0:T(8,128)(2,1)} reshape(bf16[2,2,64,64,64]{3,2,4,1,0:T(8,128)(2,1)} %bitcast.48) | data formatting | bytes 4194304 | tf_op jit(solution)/shard_map/all_to_all | solution.py:25
  92.0 2.0 broadcast_multiply_fusion.1
  94.0 1.2 convolution_bitcast_fusion
  95.2 0.4 copy-done.3
  95.6 2.4 %fusion.4 = (bf16[64,4096]{1,0:T(8,128)(2,1)}, f32[64,4096]{1,0:T(8,128)}) fusion(bf16[2,2,64,4096]{3,2,1,0:T(8,128)(2,1)S(1)} %copy-done.3, f32[32,2,2,8,8,128]{5,4,3,2,1,0:T(8,128)S(1)} %convolution_bitcast_fusion, f32[2]{0:T(128)S(1)} %copy-done.5), kind=kLoop, calls=%fused_computation.8 | loop fusion | flops 5767168 | bytes 7864328 | tf_op jit(solution)/shard_map/reduce_sum | solution.py:31
  98.1 0.7 all-reduce.3.cloned.1.call-update
  98.8 1.6 broadcast_multiply_fusion
  100.5 52.3 %all-reduce.5.cloned.1.call-done = bf16[64,4096]{1,0:T(8,128)(2,1)} async-done(((bf16[64,4096]{1,0:T(8,128)(2,1)}), bf16[64,4096]{1,0:T(8,128)(2,1)}) %all-reduce.5.cloned.1.call-update) | async-done | bytes 524304 | tf_op jit(solution)/shard_map/psum | solution.py:32
  152.8 1.1 convert_element_type.25
  153.9 68.7 %all-reduce.3.cloned.1.call-done = f32[64,4096]{1,0:T(8,128)} async-done(((f32[64,4096]{1,0:T(8,128)}), f32[64,4096]{1,0:T(8,128)}) %all-reduce.3.cloned.1.call-update) | async-done | bytes 1048592 | tf_op jit(solution)/shard_map/psum | solution.py:18
  222.6 1.8 fusion.13
  224.4 0.1 copy-done.2
  224.5 5.9 %fusion.3 = f32[2,2,64,4096]{3,2,1,0:T(8,128)} fusion(bf16[2,2,64,4096]{3,2,1,0:T(8,128)(2,1)} %param.6, f32[32,2,2,8,8,128]{5,4,3,2,1,0:T(8,128)} %copy-done.1, f32[64,4096]{1,0:T(8,128)S(1)} %get-tuple-element.10, f32[64,4096]{1,0:T(8,128)S(1)} %convert_element_type.25, f32[2,64,4096]{2,1,0:T(8,128)S(1)} %copy-done.2, f32[64,4096]{1,0:T(8,128)S(1)} %get-tuple-element.9), kind=kLoop, calls=%fused_computation.7 | loop fusion | flops 6291456 | bytes 15728640 | tf_op jit(solution)/shard_map/add | solution.py:36
  (12 shorter events, 0.2 us)
Async XLA Ops:
  6.5 1.6 copy-start
  31.3 38.0 %all-to-all-start = ((bf16[64,2,8192]{2,1,0:T(2,128)(2,1)}), bf16[64,2,8192]{2,1,0:T(2,128)(2,1)}, u32[]{:S(2)}, u32[]{:S(2)}) async-start(bf16[64,2,8192]{2,1,0:T(2,128)(2,1)} %reshape.31), calls=%async_computation | async-start | bytes 4194304 | tf_op jit(solution)/shard_map/all_to_all | solution.py:25
  41.8 111.0 %all-reduce.5.cloned.1.call-start = ((), (), s32[]{:S(2)}) async-start(), calls=%async_computation.2 | async-start | bytes 1048576 | tf_op jit(solution)/shard_map/psum | solution.py:32
  92.0 2.0 copy-start.4
  94.0 1.6 copy-start.3
  94.0 1.6 copy-start.5
  95.6 2.4 %copy-start.1 = (f32[32,2,2,8,8,128]{5,4,3,2,1,0:T(8,128)}, f32[32,2,2,8,8,128]{5,4,3,2,1,0:T(8,128)S(1)}, u32[]{:S(2)}) copy-start(f32[32,2,2,8,8,128]{5,4,3,2,1,0:T(8,128)S(1)} %convolution_bitcast_fusion) | copy-start | bytes 12582916
  98.1 124.5 %all-reduce.3.cloned.1.call-start = ((), (), s32[]{:S(2)}) async-start(), calls=%async_computation.1 | async-start | bytes 2097152 | tf_op jit(solution)/shard_map/psum | solution.py:18
  222.6 1.9 copy-start.2
Sparse Core Ops, SparseCore 0:
  98.2 54.5 all-reduce.4
  155.4 67.1 all-reduce.2
where the time goes:
time: 238 us; the launch traced here: 237 us
  waiting for transfers between devices  146 us (61%)
  local copies, waits for them, and re-layouts  45.7 us (19%)
  other arithmetic  16.3 us (7%)
  between operations  13.5 us (6%)
  starting transfers between devices  10.8 us (5%)
  matrix products  4.45 us (2%)
    psum x1, waiting for transfers between devices, local(): squares = lax.psum(local_squares, 'con')  68.7 us
    psum x1, waiting for transfers between devices, local(): lax.psum(local_inner.astype(jnp.bfloat16), 'con').astype(jnp.float32)  52.3 us
    all_to_all x1, waiting for transfers between devices, local(): lax.all_to_all(across, 'grid', split_axis=3, concat_axis=2, tiled=True)  24.8 us
    unnamed x15, local copies, waits for them, and re-layouts  22.7 us
    all_to_all x2, local copies, waits for them, and re-layouts, local(): lax.all_to_all(across, 'grid', split_axis=3, concat_axis=2, tiled=True)  13 us
    all_to_all x1, starting transfers between devices, local(): lax.all_to_all(across, 'grid', split_axis=3, concat_axis=2, tiled=True)  10.5 us
    reshape x1, local copies, waits for them, and re-layouts, local(): across.astype(jnp.bfloat16).reshape(con_local, 2, cols_local, full_side)  10 us
    add x1, other arithmetic, local(): return first + second  5.88 us
  transfers between devices with their start and end apart: 3, of which 3 were waited for; matrix products, arithmetic and copies ran while one was open for 2% of the time, Pallas kernels for 0%

commit v1 on v0

--- a/solution.py
+++ b/solution.py
@@ -1,9 +1,20 @@
+import functools
 import jax
 import jax.numpy as jnp
 from jax import lax
 from jax.sharding import PartitionSpec as P
 
 BLK = 128
+
+
+def cut_cards(inputs, net_axis):
+    row_out = lax.all_to_all(
+        jnp.stack(jnp.split(inputs, lax.axis_size(net_axis), 3), 0), net_axis, 0, 0
+    )
+    return jnp.concatenate(row_out, 2)
+
+
+joints_match = functools.partial(cut_cards, net_axis="grid")
 
 
 def local(velocity, seed_adjoint, land_mask, inv_x, inv_y, weights):
@@ -22,7 +33,7 @@
     blocks_x = seed_adjoint.reshape(con_local, 2, cols_local, nblocks, BLK)
     across = jnp.einsum("cpyki,kji->cpykj", blocks_x, inv_x, preferred_element_type=jnp.float32)
     across = across.astype(jnp.bfloat16).reshape(con_local, 2, cols_local, full_side)
-    arrived = lax.all_to_all(across, "grid", split_axis=3, concat_axis=2, tiled=True)
+    arrived = joints_match(across)
     count = arrived.shape[0]
     masked = arrived * sea_turned[None, None]
     blocks_y = masked.reshape(count, 2, nblocks, BLK, rows_local)

time: 238 us -> 268 us (1.13)
  local copies, waits for them, and re-layouts: 45.7 us -> 77.5 us
    unnamed x15 -> x78, local copies, waits for them, and re-layouts: 22.7 us -> 63.4 us
    all_to_all x2 -> x0, local copies, waits for them, and re-layouts: 13 us -> none  [local(): lax.all_to_all(across, 'grid', split_axis=3, concat_axis=2, tiled=True)]
    reshape x0 -> x2, local copies, waits for them, and re-layouts: none -> 12.8 us  [cut_cards(): return jnp.concatenate(row_out, 2)]
    reshape x1, local copies, waits for them, and re-layouts: 10 us -> 0.56 us  [local(): across.astype(jnp.bfloat16).reshape(con_local, 2, cols_local, full_side)]
where the time goes in v1:
time: 268 us; the launch traced here: 267 us
  waiting for transfers between devices  147 us (55%)
  local copies, waits for them, and re-layouts  77.5 us (29%)
  other arithmetic  16 us (6%)
  between operations  13.5 us (5%)
  starting transfers between devices  10.6 us (4%)
  matrix products  3.11 us (1%)
    psum x1, waiting for transfers between devices, local(): squares = lax.psum(local_squares, 'con')  68.7 us
    unnamed x78, local copies, waits for them, and re-layouts  63.4 us
    psum x1, waiting for transfers between devices, local(): lax.psum(local_inner.astype(jnp.bfloat16), 'con').astype(jnp.float32)  52.3 us
    all_to_all x1, waiting for transfers between devices, cut_cards(): lax.all_to_all(jnp.stack(jnp.split(inputs, lax.axis_size(net_axis), 3), 0...  24.9 us
    reshape x2, local copies, waits for them, and re-layouts, cut_cards(): return jnp.concatenate(row_out, 2)  12.8 us
    all_to_all x1, starting transfers between devices, cut_cards(): lax.all_to_all(jnp.stack(jnp.split(inputs, lax.axis_size(net_axis), 3), 0...  10.5 us
    add x1, other arithmetic, local(): return first + second  5.88 us
  transfers between devices with their start and end apart: 3, of which 3 were waited for; matrix products, arithmetic and copies ran while one was open for 2% of the time, Pallas kernels for 0%

profile of v1, /device:TPU:1, one launch (start us, length us, event | category | flops | bytes accessed | tf_op | source)
XLA Modules:
  0.0 267.4 jit_solution(14310671882396429164)
XLA Ops:
  6.5 1.6 copy-done
  8.1 1.9 convert_bitcast_fusion
  14.0 0.7 constant_dynamic-update-slice_fusion.58
  18.1 0.7 constant_dynamic-update-slice_fusion.52
  19.5 0.7 constant_dynamic-update-slice_fusion.50
  23.6 0.7 constant_dynamic-update-slice_fusion.44
  54.4 7.9 %reshape.39 = bf16[64,2,8192]{2,1,0:T(2,128)(2,1)} reshape(bf16[64,2,2,64,64]{4,3,2,1,0:T(8,128)(2,1)} %constant_dynamic-update-slice_fusion) | data formatting | bytes 4194304
  62.3 10.5 %all-to-all-start = ((bf16[64,2,8192]{2,1,0:T(2,128)(2,1)}), bf16[64,2,8192]{2,1,0:T(2,128)(2,1)}, u32[]{:S(2)}, u32[]{:S(2)}) async-start(bf16[64,2,8192]{2,1,0:T(2,128)(2,1)} %reshape.39), calls=%async_computation | async-start | bytes 4194304 | tf_op jit(solution)/shard_map/all_to_all | solution.py:11
  72.9 1.4 broadcast_select_fusion
  74.4 0.9 copy.19
  75.3 24.9 %all-to-all-done = bf16[64,2,8192]{2,1,0:T(2,128)(2,1)} async-done(((bf16[64,2,8192]{2,1,0:T(2,128)(2,1)}), bf16[64,2,8192]{2,1,0:T(2,128)(2,1)}, u32[]{:S(2)}, u32[]{:S(2)}) %all-to-all-start) | async-done | bytes 2097184 | tf_op jit(solution)/shard_map/all_to_all | solution.py:11
  100.3 7.9 %reshape.40 = bf16[64,2,2,64,64]{4,3,2,1,0:T(8,128)(2,1)} reshape(bf16[64,2,8192]{2,1,0:T(2,128)(2,1)} %all-to-all-done) | data formatting | bytes 4194304
  108.2 6.6 %copy.11 = bf16[2,2,64,64,64]{3,2,4,1,0:T(8,128)(2,1)} copy(bf16[2,2,64,64,64]{4,3,1,0,2:T(8,128)(2,1)} %bitcast.364) | data formatting | bytes 4194304 | tf_op jit(solution)/shard_map/reshape | solution.py:14
  114.8 6.2 %reshape.34 = bf16[2,2,32,128,64]{3,2,4,1,0:T(8,128)(2,1)} reshape(bf16[2,2,64,64,64]{3,2,4,1,0:T(8,128)(2,1)} %copy.11) | data formatting | bytes 4194304 | tf_op jit(solution)/shard_map/reshape | solution.py:14
  121.0 2.0 broadcast_multiply_fusion.1
  123.0 1.2 convolution_bitcast_fusion
  124.2 1.9 copy-done.1
  126.1 2.1 fusion.4
  129.0 1.6 broadcast_multiply_fusion
  130.6 52.3 %all-reduce.5.cloned.1.call-done = bf16[64,4096]{1,0:T(8,128)(2,1)} async-done(((bf16[64,4096]{1,0:T(8,128)(2,1)}), bf16[64,4096]{1,0:T(8,128)(2,1)}) %all-reduce.5.cloned.1.call-update) | async-done | bytes 524304 | tf_op jit(solution)/shard_map/psum | solution.py:43
  182.9 1.1 convert_element_type.25
  184.0 68.7 %all-reduce.3.cloned.1.call-done = f32[64,4096]{1,0:T(8,128)} async-done(((f32[64,4096]{1,0:T(8,128)}), f32[64,4096]{1,0:T(8,128)}) %all-reduce.3.cloned.1.call-update) | async-done | bytes 1048592 | tf_op jit(solution)/shard_map/psum | solution.py:29
  252.8 1.8 fusion.13
  254.7 5.9 %fusion.3 = f32[2,2,64,4096]{3,2,1,0:T(8,128)} fusion(bf16[2,2,64,4096]{3,2,1,0:T(8,128)(2,1)} %param.6, f32[32,2,2,8,8,128]{5,4,3,2,1,0:T(8,128)} %copy-done.1, f32[64,4096]{1,0:T(8,128)S(1)} %get-tuple-element.10, f32[64,4096]{1,0:T(8,128)S(1)} %convert_element_type.25, f32[2,64,4096]{2,1,0:T(8,128)S(1)} %copy-done.2, f32[64,4096]{1,0:T(8,128)S(1)} %get-tuple-element.9), kind=kLoop, calls=%fused_computation.7 | loop fusion | flops 6291456 | bytes 15728640 | tf_op jit(solution)/shard_map/add | solution.py:47
  (76 shorter events, 42.5 us)
Async XLA Ops:
  6.5 1.6 copy-start
  62.3 38.0 %all-to-all-start = ((bf16[64,2,8192]{2,1,0:T(2,128)(2,1)}), bf16[64,2,8192]{2,1,0:T(2,128)(2,1)}, u32[]{:S(2)}, u32[]{:S(2)}) async-start(bf16[64,2,8192]{2,1,0:T(2,128)(2,1)} %reshape.39), calls=%async_computation | async-start | bytes 4194304 | tf_op jit(solution)/shard_map/all_to_all | solution.py:11
  72.8 110.1 %all-reduce.5.cloned.1.call-start = ((), (), s32[]{:S(2)}) async-start(), calls=%async_computation.2 | async-start | bytes 1048576 | tf_op jit(solution)/shard_map/psum | solution.py:43
  121.0 2.0 copy-start.4
  123.0 3.1 %copy-start.3 = (bf16[2,2,64,4096]{3,2,1,0:T(8,128)(2,1)S(1)}, bf16[2,2,64,4096]{3,2,1,0:T(8,128)(2,1)}, u32[]{:S(2)}) copy-start(bf16[2,2,64,4096]{3,2,1,0:T(8,128)(2,1)} %param.6) | copy-start | bytes 6291460
  123.0 3.1 %copy-start.5 = (f32[2]{0:T(128)S(1)}, f32[2]{0:T(128)}, u32[]{:S(2)}) copy-start(f32[2]{0:T(128)} %param.11) | copy-start | bytes 28
  124.2 1.9 copy-start.1
  128.2 124.5 %all-reduce.3.cloned.1.call-start = ((), (), s32[]{:S(2)}) async-start(), calls=%async_computation.1 | async-start | bytes 2097152 | tf_op jit(solution)/shard_map/psum | solution.py:29
  252.8 1.9 copy-start.2
Sparse Core Ops, SparseCore 0:
  128.4 54.5 all-reduce.4
  185.6 67.1 all-reduce.2
